TPU v7x, 128 devices: a whole 4x4x4 slice. The times are simulated.
128 devices in a mesh: grp: 8 (over z, core), dev: 16 (over y, x).
Axes of the slice: x: 4, y: 4, z: 4, core: 2. Of those that a mesh axis runs over, the one named last changes fastest.
Arguments:
- positions: float32 [3, 131072], P(None, ('grp', 'dev')), may hold values from -3 to 3
- velocities: float32 [3, 131072], P(None, ('grp', 'dev')), may hold values from -5 to 5
- accelerations: float32 [3, 131072], P(None, ('grp', 'dev')), may hold values from -3 to 3
- jerks: float32 [3, 131072], P(None, ('grp', 'dev')), may hold values from -3 to 3
- levels: int32 [131072], P(('grp', 'dev')), may hold values from 0 to 5
- counts: int32 [2, 128], replicated, may hold values from 1 to 256, 16384 in all within a row
- active_rows: int32 [2, 32768], P(None, ('grp', 'dev')), may hold values from 0 to 1023, as said below
Outputs:
- new_positions: float32 [3, 131072], P(None, ('grp', 'dev'))
- new_velocities: float32 [3, 131072], P(None, ('grp', 'dev'))
- new_accelerations: float32 [3, 131072], P(None, ('grp', 'dev'))
- new_jerks: float32 [3, 131072], P(None, ('grp', 'dev'))
Inputs may be any that keep to these rules, and one draw needn't show every extreme that they name: In each step the 128 counts sum to exactly 16384 and the largest of them is exactly 256. `active_rows`: for each step and device, the 256 entries of the device's slots are distinct indices of that device's own stars; only the first counts of them are live.
All inputs are finite; a program needn't handle non-finite values.
Results may differ from a plain program's by a relative error of at most 0.00022.
Values sent between devices are 32-bit elements; how exact they have to be, the bound alone decides.
No kernel may reach another device: no remote copies, remote signals or barrier semaphores. Data moves between devices by JAX's collectives and lax.ppermute only.
A program may use at most 128 MiB of HBM per device.

v0:
```python
import math
import jax
import jax.numpy as jnp
from jax import lax
from jax.sharding import PartitionSpec as P

tick_length = 1.0 / 128.0


def pair_block(targets, src_pos, src_vel, mass, soft_sq):
    gap_x = src_pos[0][None, :] - targets[0][:, None]
    gap_y = src_pos[1][None, :] - targets[1][:, None]
    gap_z = src_pos[2][None, :] - targets[2][:, None]
    drift_x = src_vel[0][None, :] - targets[3][:, None]
    drift_y = src_vel[1][None, :] - targets[4][:, None]
    drift_z = src_vel[2][None, :] - targets[5][:, None]
    squared = gap_x * gap_x + gap_y * gap_y + gap_z * gap_z + soft_sq
    inverse = lax.rsqrt(squared)
    weight = mass * inverse * inverse * inverse
    along = 3.0 * (gap_x * drift_x + gap_y * drift_y + gap_z * drift_z) * inverse * inverse
    return jnp.stack(
        [
            jnp.sum(weight * gap_x, axis=1),
            jnp.sum(weight * gap_y, axis=1),
            jnp.sum(weight * gap_z, axis=1),
            jnp.sum(weight * (drift_x - along * gap_x), axis=1),
            jnp.sum(weight * (drift_y - along * gap_y), axis=1),
            jnp.sum(weight * (drift_z - along * gap_z), axis=1),
        ]
    )


def block_terms(packed, src_pos, src_vel, mass, soft_sq):
    width, total = packed.shape
    block = math.gcd(total, 2048)
    grouped = packed.reshape(width, total // block, block).transpose(1, 0, 2)
    result = lax.map(lambda targets: pair_block(targets, src_pos, src_vel, mass, soft_sq), grouped)
    return result.transpose(1, 0, 2).reshape(width, total)


def predict(positions, velocities, accelerations, jerks, elapsed):
    span = elapsed[None, :]
    pred_pos = (
        positions
        + span * velocities
        + 0.5 * span * span * accelerations
        + span * span * span / 6.0 * jerks
    )
    pred_vel = velocities + span * accelerations + 0.5 * span * span * jerks
    return (pred_pos, pred_vel)


def correct(old_pos, old_vel, old_acc, old_jerk, force, jerk_new, span):
    span = span[None, :]
    new_vel = old_vel + 0.5 * span * (old_acc + force) + span * span / 12.0 * (old_jerk - jerk_new)
    new_pos = old_pos + 0.5 * span * (old_vel + new_vel) + span * span / 12.0 * (old_acc - force)
    return (new_pos, new_vel)


def shards(positions, velocities, accelerations, jerks, levels, counts, active_rows):
    devices_all = lax.axis_size("grp") * lax.axis_size("dev")
    my_rank = lax.axis_index("grp") * lax.axis_size("dev") + lax.axis_index("dev")
    star_dev = positions.shape[1]
    slot_cap = active_rows.shape[1]
    stars_all = star_dev * devices_all
    live_all = stars_all // 8
    mass = 1.0 / stars_all
    soft_sq = 0.0004 * (131072.0 / stars_all) ** (2.0 / 3.0)
    chunks = 4
    chunk = live_all // chunks
    last_time = -(jnp.left_shift(jnp.int32(1), levels) - 1).astype(jnp.float32) * tick_length
    for step in range(active_rows.shape[0]):
        now = (step + 1) * tick_length
        pred_pos, pred_vel = predict(positions, velocities, accelerations, jerks, now - last_time)
        rows = active_rows[step]
        targets = jnp.concatenate([pred_pos[:, rows], pred_vel[:, rows]], axis=0)
        step_counts = counts[step]
        own_count = step_counts[my_rank]
        inclusive = jnp.cumsum(step_counts).astype(jnp.int32)
        first = inclusive - step_counts
        place = jnp.arange(live_all, dtype=jnp.int32)
        owner = jnp.sum((inclusive[None, :] <= place[:, None]).astype(jnp.int32), axis=1)
        owner = jnp.minimum(owner, devices_all - 1)
        slot = owner * slot_cap + place - first[owner]
        gathered = lax.all_gather(targets[None], ("grp", "dev"), axis=0, tiled=True)
        flat = gathered.transpose(1, 0, 2).reshape(6, devices_all * slot_cap)
        compact = flat[:, slot]
        parts = []
        summed = None
        for c in range(chunks):
            piece = compact[:, c * chunk : (c + 1) * chunk]
            terms = block_terms(piece, pred_pos, pred_vel, mass, soft_sq)
            if summed is not None:
                terms, summed = lax.optimization_barrier((terms, summed))
                parts.append(summed)
            summed = lax.psum(terms, ("grp", "dev"))
        parts.append(summed)
        parts.append(jnp.zeros((6, slot_cap), jnp.float32))
        totals = jnp.concatenate(parts, axis=1)
        own = lax.dynamic_slice_in_dim(totals, first[my_rank], slot_cap, 1)
        span = now - last_time[rows]
        new_pos, new_vel = correct(
            positions[:, rows],
            velocities[:, rows],
            accelerations[:, rows],
            jerks[:, rows],
            own[:3],
            own[3:],
            span,
        )
        live = jnp.arange(slot_cap, dtype=jnp.int32) < own_count
        target = jnp.where(live, rows, star_dev)
        positions = positions.at[:, target].set(new_pos, mode="drop")
        velocities = velocities.at[:, target].set(new_vel, mode="drop")
        accelerations = accelerations.at[:, target].set(own[:3], mode="drop")
        jerks = jerks.at[:, target].set(own[3:], mode="drop")
        last_time = last_time.at[target].set(now, mode="drop")
    return (positions, velocities, accelerations, jerks)


def solution(mesh):
    placed = (
        P(None, ("grp", "dev")),
        P(None, ("grp", "dev")),
        P(None, ("grp", "dev")),
        P(None, ("grp", "dev")),
        P(("grp", "dev")),
        P(),
        P(None, ("grp", "dev")),
    )
    return jax.shard_map(
        shards,
        mesh=mesh,
        in_specs=placed,
        out_specs=(
            P(None, ("grp", "dev")),
            P(None, ("grp", "dev")),
            P(None, ("grp", "dev")),
            P(None, ("grp", "dev")),
        ),
        check_vma=False,
    )
```

profile of v0, /device:TPU:1, one launch (start us, length us, event | category | flops | bytes accessed | tf_op | source)
XLA Modules:
  0.0 1731.8 jit_solution(9103468403013295511)
XLA Ops:
  8.6 2.6 compare_select_fusion.4
  14.8 63.9 %all-gather.2 = f32[128,6,256]{2,1,0:T(8,128)S(1)} all-gather(f32[1,6,256]{2,1,0:T(8,128)S(1)} %maximum_bitcast_fusion), channel_id=2, replica_groups=mesh['grp'=8,'dev'=16] {'grp','dev'}, dimensions={0}, use_global_device_ids=true | all-gather | bytes 792576 | tf_op jit(solution)/shard_map/all_gather | solution.py:85
  78.7 8.4 copy.253
  87.8 2.3 convert_reduce_fusion.1
  90.3 97.2 %gather_fusion.6 = s32[16384]{0:T(1024)S(1)} fusion(s32[128]{0:T(128)S(1)} %get-tuple-element.734, s32[16384]{0:T(1024)S(1)} %broadcast_clamp_fusion.3), kind=kCustom, calls=%fused_computation.6 | custom fusion | bytes 196608 | tf_op jit(solution)/shard_map/gather | solution.py:84
  187.7 60.2 %gather_fusion.7 = f32[16384,6]{1,0:T(8,128)} fusion(f32[6,32768]{0,1:T(8,128)} %bitcast.632, s32[16384]{0:T(1024)S(1)} %broadcast_clamp_fusion.1), kind=kCustom, calls=%fused_computation.7 | custom fusion | bytes 851968 | tf_op jit(solution)/shard_map/gather | solution.py:87
  247.9 6.2 fusion.167
  256.3 32.8 %while.81 = (s32[]{:T(128)}, f32[2,6,2048]{2,1,0:T(8,128)S(1)}, f32[3,1024]{1,0:T(4,128)S(1)}, f32[2,6,2048]{2,1,0:T(8,128)S(1)}, f32[3,1024]{1,0:T(4,128)S(1)},...) while((s32[]{:T(128)}, f32[2,6,2048]{2,1,0:T(8,128)S(1)}, ...), condition=%wide.region_17.18_spmd, body=%wide.region_10.17_spmd.sunk | while | flops 85970952 | bytes 499925 | solution.py:37
  256.4 16.2 fusion.187
  272.8 16.2 fusion.187
  290.1 2.3 convert_reduce_fusion
  292.5 2.2 copy.255
  294.7 32.8 %while.80 = (s32[]{:T(128)}, f32[2,6,2048]{2,1,0:T(8,128)S(1)}, f32[3,1024]{1,0:T(4,128)S(1)}, f32[2,6,2048]{2,1,0:T(8,128)S(1)}, f32[3,1024]{1,0:T(4,128)S(1)},...) while((s32[]{:T(128)}, f32[2,6,2048]{2,1,0:T(8,128)S(1)}, ...), condition=%wide.region_9.10_spmd, body=%wide.region_2.9_spmd.sunk | while | flops 85970952 | bytes 499925 | solution.py:37
  294.8 16.2 fusion.185
  311.2 16.2 fusion.185
  327.5 2.3 copy.257
  329.8 32.8 %while.82 = (s32[]{:T(128)}, f32[2,6,2048]{2,1,0:T(8,128)S(1)}, f32[3,1024]{1,0:T(4,128)S(1)}, f32[2,6,2048]{2,1,0:T(8,128)S(1)}, f32[3,1024]{1,0:T(4,128)S(1)},...) while((s32[]{:T(128)}, f32[2,6,2048]{2,1,0:T(8,128)S(1)}, ...), condition=%wide.region_26.27_spmd, body=%wide.region_19.26_spmd.sunk | while | flops 85970952 | bytes 499925 | solution.py:37
  329.9 16.2 fusion.189
  346.4 16.2 fusion.189
  363.3 32.9 %while.83 = (s32[]{:T(128)}, f32[2,6,2048]{2,1,0:T(8,128)S(1)}, f32[3,1024]{1,0:T(4,128)S(1)}, f32[2,6,2048]{2,1,0:T(8,128)S(1)}, f32[3,1024]{1,0:T(4,128)S(1)},...) while((s32[]{:T(128)}, f32[2,6,2048]{2,1,0:T(8,128)S(1)}, ...), condition=%wide.region_35.36_spmd, body=%wide.region_28.35_spmd.sunk | while | flops 85970952 | bytes 499925 | solution.py:37
  363.4 16.2 fusion.191
  379.9 16.2 fusion.191
  399.8 97.2 %gather_fusion.15 = s32[16384]{0:T(1024)S(1)} fusion(s32[128]{0:T(128)S(1)} %get-tuple-element.733, s32[16384]{0:T(1024)S(1)} %broadcast_clamp_fusion.2), kind=kCustom, calls=%fused_computation.15 | custom fusion | bytes 196608 | tf_op jit(solution)/shard_map/gather | solution.py:84
  509.3 137.8 %all-reduce.11.cloned.1.call-done = f32[6,4096]{1,0:T(8,128)} async-done(((f32[6,4096]{1,0:T(8,128)}), f32[6,4096]{1,0:T(8,128)}) %all-reduce.11.cloned.1.call-update) | async-done | bytes 98320 | tf_op jit(solution)/shard_map/psum | solution.py:96
  648.1 141.3 %all-reduce.13.cloned.1.call-done = f32[6,4096]{1,0:T(8,128)} async-done(((f32[6,4096]{1,0:T(8,128)}), f32[6,4096]{1,0:T(8,128)}) %all-reduce.13.cloned.1.call-update) | async-done | bytes 98320 | tf_op jit(solution)/shard_map/psum | solution.py:96
  790.4 141.8 %all-reduce.15.cloned.1.call-done = f32[6,4096]{1,0:T(8,128)} async-done(((f32[6,4096]{1,0:T(8,128)}), f32[6,4096]{1,0:T(8,128)}) %all-reduce.15.cloned.1.call-update) | async-done | bytes 98320 | tf_op jit(solution)/shard_map/psum | solution.py:96
  941.9 59.0 %all-gather.3 = f32[128,6,256]{2,1,0:T(8,128)S(1)} all-gather(f32[1,6,256]{2,1,0:T(8,128)S(1)} %maximum_bitcast_fusion.1), channel_id=3, replica_groups=mesh['grp'=8,'dev'=16] {'grp','dev'}, dimensions={0}, use_global_device_ids=true | all-gather | bytes 792576 | tf_op jit(solution)/shard_map/all_gather | solution.py:85
  1000.9 8.4 copy.274
  1009.3 60.2 %gather_fusion.16 = f32[16384,6]{1,0:T(8,128)} fusion(f32[6,32768]{0,1:T(8,128)} %bitcast.633, s32[16384]{0:T(1024)S(1)} %broadcast_clamp_fusion), kind=kCustom, calls=%fused_computation.16 | custom fusion | bytes 851968 | tf_op jit(solution)/shard_map/gather | solution.py:87
  1069.4 6.2 fusion.166
  1077.9 32.8 %while.84 = (s32[]{:T(128)}, f32[2,6,2048]{2,1,0:T(8,128)S(1)}, f32[3,1024]{1,0:T(4,128)S(1)}, f32[2,6,2048]{2,1,0:T(8,128)S(1)}, f32[3,1024]{1,0:T(4,128)S(1)},...) while((s32[]{:T(128)}, f32[2,6,2048]{2,1,0:T(8,128)S(1)}, ...), condition=%wide.region_52.53_spmd, body=%wide.region_45.52_spmd.sunk | while | flops 85970952 | bytes 499925 | solution.py:37
  1078.0 16.2 fusion.193
  1094.4 16.2 fusion.193
  1110.7 2.3 copy.279
  1113.6 34.0 %while.85 = (s32[]{:T(128)}, f32[2,6,2048]{2,1,0:T(8,128)}, f32[3,1024]{1,0:T(4,128)S(1)}, f32[2,6,2048]{2,1,0:T(8,128)S(1)}, f32[3,1024]{1,0:T(4,128)S(1)}, /*i...) while((s32[]{:T(128)}, f32[2,6,2048]{2,1,0:T(8,128)}, f32[3,1024]{1,0:T(4,128)S(1)}, ...), condition=%wide.region_60.61_spmd, body=%wide.region_53.60_spmd.sunk | while | flops 85970952 | bytes 483541 | solution.py:37
  1113.7 16.2 fusion.195
  1130.7 16.2 fusion.195
  1147.9 2.2 copy.282
  1150.1 32.8 %while.86 = (s32[]{:T(128)}, f32[2,6,2048]{2,1,0:T(8,128)S(1)}, f32[3,1024]{1,0:T(4,128)S(1)}, f32[2,6,2048]{2,1,0:T(8,128)S(1)}, f32[3,1024]{1,0:T(4,128)S(1)},...) while((s32[]{:T(128)}, f32[2,6,2048]{2,1,0:T(8,128)S(1)}, ...), condition=%wide.region_69.70_spmd, body=%wide.region_62.69_spmd.sunk | while | flops 85970952 | bytes 499925 | solution.py:37
  1150.2 16.2 fusion.197
  1166.6 16.2 fusion.197
  1183.7 32.8 %while.87 = (s32[]{:T(128)}, f32[2,6,2048]{2,1,0:T(8,128)S(1)}, f32[3,1024]{1,0:T(4,128)S(1)}, f32[2,6,2048]{2,1,0:T(8,128)S(1)}, f32[3,1024]{1,0:T(4,128)S(1)},...) while((s32[]{:T(128)}, f32[2,6,2048]{2,1,0:T(8,128)S(1)}, ...), condition=%wide.region_78.79_spmd, body=%wide.region_71.78_spmd.sunk | while | flops 85970952 | bytes 499925 | solution.py:37
  1183.8 16.2 fusion.199
  1200.2 16.2 fusion.199
  1219.8 66.7 %all-reduce.17.cloned.1.call-done = f32[6,4096]{1,0:T(8,128)} async-done(((f32[6,4096]{1,0:T(8,128)}), f32[6,4096]{1,0:T(8,128)}) %all-reduce.17.cloned.1.call-update) | async-done | bytes 98320 | tf_op jit(solution)/shard_map/psum | solution.py:96
  1287.5 141.8 %all-reduce.19.cloned.1.call-done = f32[6,4096]{1,0:T(8,128)} async-done(((f32[6,4096]{1,0:T(8,128)}), f32[6,4096]{1,0:T(8,128)}) %all-reduce.19.cloned.1.call-update) | async-done | bytes 98320 | tf_op jit(solution)/shard_map/psum | solution.py:96
  1430.3 141.2 %all-reduce.21.cloned.1.call-done = f32[6,4096]{1,0:T(8,128)} async-done(((f32[6,4096]{1,0:T(8,128)}), f32[6,4096]{1,0:T(8,128)}) %all-reduce.21.cloned.1.call-update) | async-done | bytes 98320 | tf_op jit(solution)/shard_map/psum | solution.py:96
  1572.5 142.0 %all-reduce.23.cloned.1.call-done = f32[6,4096]{1,0:T(8,128)} async-done(((f32[6,4096]{1,0:T(8,128)}), f32[6,4096]{1,0:T(8,128)}) %all-reduce.23.cloned.1.call-update) | async-done | bytes 98320 | tf_op jit(solution)/shard_map/psum | solution.py:96
  (234 shorter events, 57.5 us)
Async XLA Ops:
  7.2 501.2 %all-reduce.9.cloned.1.call-start = ((), (), s32[]{:S(2)}) async-start(), calls=%async_computation | async-start | bytes 262144 | tf_op jit(solution)/shard_map/psum | solution.py:96
  78.7 11.5 copy-start.18
  289.1 0.6 copy-start.5
  289.8 357.4 %all-reduce.11.cloned.1.call-start = ((), (), s32[]{:S(2)}) async-start(), calls=%async_computation.1 | async-start | bytes 262144 | tf_op jit(solution)/shard_map/psum | solution.py:96
  327.5 2.3 copy-start.6
  362.7 0.7 copy-start.7
  396.2 100.8 %copy-start.8 = (f32[2,6,2048]{2,1,0:T(8,128)}, f32[2,6,2048]{2,1,0:T(8,128)S(1)}, u32[]{:S(2)}) copy-start(f32[2,6,2048]{2,1,0:T(8,128)S(1)} %get-tuple-element.238) | copy-start | bytes 294916
  397.6 543.1 %copy-start.15 = (s32[1024]{0:T(1024)}, s32[1024]{0:T(1024)S(1)}, u32[]{:S(2)}) copy-start(s32[1024]{0:T(1024)S(1)} %pad_clamp_fusion) | copy-start | bytes 12292
  399.7 99.4 %copy-start.11 = (f32[3,1024]{1,0:T(4,128)S(1)}, f32[3,1024]{1,0:T(4,128)}, u32[]{:S(2)}) copy-start(f32[3,1024]{1,0:T(4,128)} %param.23) | copy-start | bytes 36868
  399.7 99.6 %copy-start.12 = (f32[3,1024]{1,0:T(4,128)S(1)}, f32[3,1024]{1,0:T(4,128)}, u32[]{:S(2)}) copy-start(f32[3,1024]{1,0:T(4,128)} %param.25) | copy-start | bytes 36868
  399.7 99.8 %copy-start.13 = (f32[3,1024]{1,0:T(4,128)S(1)}, f32[3,1024]{1,0:T(4,128)}, u32[]{:S(2)}) copy-start(f32[3,1024]{1,0:T(4,128)} %param.24) | copy-start | bytes 36868
  399.7 100.7 %copy-start.14 = (f32[3,1024]{1,0:T(4,128)S(1)}, f32[3,1024]{1,0:T(4,128)}, u32[]{:S(2)}) copy-start(f32[3,1024]{1,0:T(4,128)} %param.26) | copy-start | bytes 36868
  508.4 281.0 %all-reduce.13.cloned.1.call-start = ((), (), s32[]{:S(2)}) async-start(), calls=%async_computation.2 | async-start | bytes 262144 | tf_op jit(solution)/shard_map/psum | solution.py:96
  647.2 285.0 %all-reduce.15.cloned.1.call-start = ((), (), s32[]{:S(2)}) async-start(), calls=%async_computation.3 | async-start | bytes 262144 | tf_op jit(solution)/shard_map/psum | solution.py:96
  789.4 497.1 %all-reduce.17.cloned.1.call-start = ((), (), s32[]{:S(2)}) async-start(), calls=%async_computation.4 | async-start | bytes 262144 | tf_op jit(solution)/shard_map/psum | solution.py:96
  934.7 74.5 %copy-start.2 = (f32[3,1024]{0,1:T(8,128)}, f32[3,1024]{0,1:T(8,128)S(1)}, u32[]{:S(2)}) copy-start(f32[3,1024]{0,1:T(8,128)S(1)} %scatter_fusion) | copy-start | bytes 36868
  936.3 73.0 %copy-start = (f32[3,1024]{0,1:T(8,128)}, f32[3,1024]{0,1:T(8,128)S(1)}, u32[]{:S(2)}) copy-start(f32[3,1024]{0,1:T(8,128)S(1)} %scatter_fusion.3) | copy-start | bytes 36868
  1110.7 2.9 copy-start.9
  1147.6 281.7 %all-reduce.19.cloned.1.call-start = ((), (), s32[]{:S(2)}) async-start(), calls=%async_computation.5 | async-start | bytes 262144 | tf_op jit(solution)/shard_map/psum | solution.py:96
  1183.0 0.7 copy-start.10
  1183.6 32.9 %copy-start.1 = (f32[3,1024]{0,1:T(8,128)S(1)}, f32[3,1024]{0,1:T(8,128)}, u32[]{:S(2)}) copy-start(f32[3,1024]{0,1:T(8,128)} %copy-done) | copy-start | bytes 36868
  1183.6 32.9 %copy-start.16 = (s32[1024]{0:T(1024)S(1)}, s32[1024]{0:T(1024)}, u32[]{:S(2)}) copy-start(s32[1024]{0:T(1024)} %copy-done.15) | copy-start | bytes 12292
  1183.6 34.3 %copy-start.3 = (f32[3,1024]{0,1:T(8,128)S(1)}, f32[3,1024]{0,1:T(8,128)}, u32[]{:S(2)}) copy-start(f32[3,1024]{0,1:T(8,128)} %copy-done.2) | copy-start | bytes 36868
  1183.6 531.7 %copy-start.19 = (f32[256]{0:T(256)S(1)}, f32[256]{0:T(256)}, u32[]{:S(2)}) copy-start(f32[256]{0:T(256)} %get-tuple-element.731) | copy-start | bytes 3076
  1183.6 531.7 %copy-start.20 = (f32[256]{0:T(256)S(1)}, f32[256]{0:T(256)}, u32[]{:S(2)}) copy-start(f32[256]{0:T(256)} %get-tuple-element.732) | copy-start | bytes 3076
  1183.7 531.9 %copy-start.17 = (s32[256,1]{0,1:T(1,128)S(1)}, s32[256,1]{0,1:T(1,128)}, u32[]{:S(2)}) copy-start(s32[256,1]{0,1:T(1,128)} %get-tuple-element.729) | copy-start | bytes 3076
  1216.5 355.0 %copy-start.4 = (f32[2,6,2048]{2,1,0:T(8,128)}, f32[2,6,2048]{2,1,0:T(8,128)S(1)}, u32[]{:S(2)}) copy-start(f32[2,6,2048]{2,1,0:T(8,128)S(1)} %get-tuple-element.248) | copy-start | bytes 294916
  1286.5 285.0 %all-reduce.21.cloned.1.call-start = ((), (), s32[]{:S(2)}) async-start(), calls=%async_computation.6 | async-start | bytes 262144 | tf_op jit(solution)/shard_map/psum | solution.py:96
  1429.3 285.1 %all-reduce.23.cloned.1.call-start = ((), (), s32[]{:S(2)}) async-start(), calls=%async_computation.7 | async-start | bytes 262144 | tf_op jit(solution)/shard_map/psum | solution.py:96
Sparse Core Ops, SparseCore 0:
  289.9 138.5 all-reduce.8
  508.5 138.5 all-reduce.10
  651.9 137.4 all-reduce.12
  794.7 137.4 all-reduce.14
  1147.8 138.6 all-reduce.16
  1291.8 137.4 all-reduce.18
  1434.0 137.4 all-reduce.20
  1577.0 137.4 all-reduce.22
where the time goes:
time: 1740 us; the launch traced here: 1730 us
  waiting for transfers between devices  913 us (52%)
  local copies, waits for them, and re-layouts  405 us (23%)
  other arithmetic  270 us (16%)
  blocking collectives  123 us (7%)
  between operations  19 us (1%)
    psum x8, waiting for transfers between devices, shards(): summed = lax.psum(terms, ('grp', 'dev'))  913 us
    reduce_sum x16, other arithmetic, pair_block(): jnp.sum(weight * (drift_z - along * gap_z), axis=1)  259 us
    gather x2, local copies, waits for them, and re-layouts, shards(): slot = owner * slot_cap + place - first[owner]  194 us
    all_gather x2, blocking collectives, shards(): gathered = lax.all_gather(targets[None], ('grp', 'dev'), axis=0, tiled=True)  123 us
    gather x2, local copies, waits for them, and re-layouts, shards(): compact = flat[:, slot]  120 us
  transfers between devices with their start and end apart: 8, of which 7 were waited for; matrix products, arithmetic and copies ran while one was open for 17% of the time, Pallas kernels for 0%

commit v1 on v0

--- a/solution.py
+++ b/solution.py
@@ -93,7 +93,7 @@
             if summed is not None:
                 terms, summed = lax.optimization_barrier((terms, summed))
                 parts.append(summed)
-            summed = lax.psum(terms, ("grp", "dev"))
+            summed = lax.psum(lax.psum(terms, "dev"), "grp")
         parts.append(summed)
         parts.append(jnp.zeros((6, slot_cap), jnp.float32))
         totals = jnp.concatenate(parts, axis=1)

time: 1740 us -> 1770 us (1.017)
  waiting for transfers between devices: 913 us -> 936 us
    psum x8 -> x16, waiting for transfers between devices: 913 us -> 936 us  [shards(): summed = lax.psum(lax.psum(terms, 'dev'), 'grp')]
  transfers between devices with their start and end apart: 8 -> 16, of which waited for: 7 -> 15; matrix products, arithmetic and copies ran while one was open for 17% -> 19% of each run, Pallas kernels for 0% -> 0%
where the time goes in v1:
time: 1770 us
  waiting for transfers between devices  936 us (53%)
  local copies, waits for them, and re-layouts  408 us (23%)
  other arithmetic  274 us (15%)
  blocking collectives  126 us (7%)
  between operations  18.9 us (1%)
    psum x16, waiting for transfers between devices, shards(): summed = lax.psum(lax.psum(terms, 'dev'), 'grp')  936 us
    reduce_sum x16, other arithmetic, pair_block(): jnp.sum(weight * (drift_z - along * gap_z), axis=1)  262 us
    gather x2, local copies, waits for them, and re-layouts, shards(): slot = owner * slot_cap + place - first[owner]  194 us
    all_gather x2, blocking collectives, shards(): gathered = lax.all_gather(targets[None], ('grp', 'dev'), axis=0, tiled=True)  126 us
    gather x2, local copies, waits for them, and re-layouts, shards(): compact = flat[:, slot]  120 us
  transfers between devices with their start and end apart: 16, of which 15 were waited for; matrix products, arithmetic and copies ran while one was open for 19% of the time, Pallas kernels for 0%

profile of v1, /device:TPU:1, one launch (start us, length us, event | category | flops | bytes accessed | tf_op | source)
XLA Modules:
  0.0 1766.1 jit_solution(5579851974811496018)
XLA Ops:
  14.8 63.9 %all-gather.2 = f32[128,6,256]{2,1,0:T(8,128)S(1)} all-gather(f32[1,6,256]{2,1,0:T(8,128)S(1)} %maximum_bitcast_fusion), channel_id=2, replica_groups=mesh['grp'=8,'dev'=16] {'grp','dev'}, dimensions={0}, use_global_device_ids=true | all-gather | bytes 792576 | tf_op jit(solution)/shard_map/all_gather | solution.py:85
  78.7 8.4 copy.253
  90.3 97.2 %gather_fusion.6 = s32[16384]{0:T(1024)S(1)} fusion(s32[128]{0:T(128)S(1)} %get-tuple-element.734, s32[16384]{0:T(1024)S(1)} %broadcast_clamp_fusion.3), kind=kCustom, calls=%fused_computation.6 | custom fusion | bytes 196608 | tf_op jit(solution)/shard_map/gather | solution.py:84
  187.7 60.2 %gather_fusion.7 = f32[16384,6]{1,0:T(8,128)} fusion(f32[6,32768]{0,1:T(8,128)} %bitcast.632, s32[16384]{0:T(1024)S(1)} %broadcast_clamp_fusion.1), kind=kCustom, calls=%fused_computation.7 | custom fusion | bytes 851968 | tf_op jit(solution)/shard_map/gather | solution.py:87
  256.3 32.9 %while.81 = (s32[]{:T(128)}, f32[2,6,2048]{2,1,0:T(8,128)S(1)}, f32[3,1024]{1,0:T(4,128)S(1)}, f32[2,6,2048]{2,1,0:T(8,128)S(1)}, f32[3,1024]{1,0:T(4,128)S(1)},...) while((s32[]{:T(128)}, f32[2,6,2048]{2,1,0:T(8,128)S(1)}, ...), condition=%wide.region_17.18_spmd, body=%wide.region_10.17_spmd.sunk | while | flops 85970952 | bytes 499925 | solution.py:37
  256.4 16.2 fusion.187
  272.8 16.2 fusion.187
  294.9 32.9 %while.80 = (s32[]{:T(128)}, f32[2,6,2048]{2,1,0:T(8,128)S(1)}, f32[3,1024]{1,0:T(4,128)S(1)}, f32[2,6,2048]{2,1,0:T(8,128)S(1)}, f32[3,1024]{1,0:T(4,128)S(1)},...) while((s32[]{:T(128)}, f32[2,6,2048]{2,1,0:T(8,128)S(1)}, ...), condition=%wide.region_9.10_spmd, body=%wide.region_2.9_spmd.sunk | while | flops 85970952 | bytes 499925 | solution.py:37
  295.0 16.2 fusion.185
  311.4 16.2 fusion.185
  330.1 32.8 %while.82 = (s32[]{:T(128)}, f32[2,6,2048]{2,1,0:T(8,128)S(1)}, f32[3,1024]{1,0:T(4,128)S(1)}, f32[2,6,2048]{2,1,0:T(8,128)S(1)}, f32[3,1024]{1,0:T(4,128)S(1)},...) while((s32[]{:T(128)}, f32[2,6,2048]{2,1,0:T(8,128)S(1)}, ...), condition=%wide.region_27.28_spmd, body=%wide.region_20.27_spmd.sunk | while | flops 85970952 | bytes 499925 | solution.py:37
  330.2 16.2 fusion.189
  346.6 16.2 fusion.189
  363.6 32.8 %while.83 = (s32[]{:T(128)}, f32[2,6,2048]{2,1,0:T(8,128)S(1)}, f32[3,1024]{1,0:T(4,128)S(1)}, f32[2,6,2048]{2,1,0:T(8,128)S(1)}, f32[3,1024]{1,0:T(4,128)S(1)},...) while((s32[]{:T(128)}, f32[2,6,2048]{2,1,0:T(8,128)S(1)}, ...), condition=%wide.region_37.38_spmd, body=%wide.region_30.37_spmd.sunk | while | flops 85970952 | bytes 499925 | solution.py:37
  363.7 16.2 fusion.191
  380.1 16.2 fusion.191
  396.6 97.2 %gather_fusion.15 = s32[16384]{0:T(1024)S(1)} fusion(s32[128]{0:T(128)S(1)} %get-tuple-element.733, s32[16384]{0:T(1024)S(1)} %broadcast_clamp_fusion.2), kind=kCustom, calls=%fused_computation.15 | custom fusion | bytes 196608 | tf_op jit(solution)/shard_map/gather | solution.py:84
  496.9 53.2 %all-reduce.19.cloned.1.call-done = f32[6,4096]{1,0:T(8,128)} async-done(((f32[6,4096]{1,0:T(8,128)}), f32[6,4096]{1,0:T(8,128)}) %all-reduce.19.cloned.1.call-update) | async-done | bytes 98320 | tf_op jit(solution)/shard_map/psum | solution.py:96
  550.1 84.6 %all-reduce.21.cloned.1.call-done = f32[6,4096]{1,0:T(8,128)} async-done(((f32[6,4096]{1,0:T(8,128)}), f32[6,4096]{1,0:T(8,128)}) %all-reduce.21.cloned.1.call-update) | async-done | bytes 98320 | tf_op jit(solution)/shard_map/psum | solution.py:96
  641.8 53.6 %all-reduce.23.cloned.1.call-done = f32[6,4096]{1,0:T(8,128)} async-done(((f32[6,4096]{1,0:T(8,128)}), f32[6,4096]{1,0:T(8,128)}) %all-reduce.23.cloned.1.call-update) | async-done | bytes 98320 | tf_op jit(solution)/shard_map/psum | solution.py:96
  695.4 84.4 %all-reduce.25.cloned.1.call-done = f32[6,4096]{1,0:T(8,128)} async-done(((f32[6,4096]{1,0:T(8,128)}), f32[6,4096]{1,0:T(8,128)}) %all-reduce.25.cloned.1.call-update) | async-done | bytes 98320 | tf_op jit(solution)/shard_map/psum | solution.py:96
  780.9 59.6 %all-reduce.27.cloned.1.call-done = f32[6,4096]{1,0:T(8,128)} async-done(((f32[6,4096]{1,0:T(8,128)}), f32[6,4096]{1,0:T(8,128)}) %all-reduce.27.cloned.1.call-update) | async-done | bytes 98320 | tf_op jit(solution)/shard_map/psum | solution.py:96
  841.5 83.7 %all-reduce.29.cloned.1.call-done = f32[6,4096]{1,0:T(8,128)} async-done(((f32[6,4096]{1,0:T(8,128)}), f32[6,4096]{1,0:T(8,128)}) %all-reduce.29.cloned.1.call-update) | async-done | bytes 98320 | tf_op jit(solution)/shard_map/psum | solution.py:96
  926.1 59.8 %all-reduce.31.cloned.1.call-done = f32[6,4096]{1,0:T(8,128)} async-done(((f32[6,4096]{1,0:T(8,128)}), f32[6,4096]{1,0:T(8,128)}) %all-reduce.31.cloned.1.call-update) | async-done | bytes 98320 | tf_op jit(solution)/shard_map/psum | solution.py:96
  995.6 62.4 %all-gather.3 = f32[128,6,256]{2,1,0:T(8,128)S(1)} all-gather(f32[1,6,256]{2,1,0:T(8,128)S(1)} %maximum_bitcast_fusion.1), channel_id=3, replica_groups=mesh['grp'=8,'dev'=16] {'grp','dev'}, dimensions={0}, use_global_device_ids=true | all-gather | bytes 792576 | tf_op jit(solution)/shard_map/all_gather | solution.py:85
  1058.0 8.4 copy.274
  1066.4 60.2 %gather_fusion.16 = f32[16384,6]{1,0:T(8,128)} fusion(f32[6,32768]{0,1:T(8,128)} %bitcast.633, s32[16384]{0:T(1024)S(1)} %broadcast_clamp_fusion), kind=kCustom, calls=%fused_computation.16 | custom fusion | bytes 851968 | tf_op jit(solution)/shard_map/gather | solution.py:87
  1126.5 6.2 fusion.166
  1135.0 35.4 %while.85 = (s32[]{:T(128)}, f32[2,6,2048]{2,1,0:T(8,128)S(1)}, f32[3,1024]{1,0:T(4,128)S(1)}, f32[2,6,2048]{2,1,0:T(8,128)S(1)}, f32[3,1024]{1,0:T(4,128)S(1)},...) while((s32[]{:T(128)}, f32[2,6,2048]{2,1,0:T(8,128)S(1)}, ...), condition=%wide.region_64.65_spmd, body=%wide.region_57.64_spmd.sunk | while | flops 85970952 | bytes 499925 | solution.py:37
  1135.1 16.8 fusion.195
  1152.8 16.8 fusion.195
  1175.4 75.3 %all-reduce.33.cloned.1.call-done = f32[6,4096]{1,0:T(8,128)} async-done(((f32[6,4096]{1,0:T(8,128)}), f32[6,4096]{1,0:T(8,128)}) %all-reduce.33.cloned.1.call-update) | async-done | bytes 98320 | tf_op jit(solution)/shard_map/psum | solution.py:96
  1251.0 35.4 %while.84 = (s32[]{:T(128)}, f32[2,6,2048]{2,1,0:T(8,128)S(1)}, f32[3,1024]{1,0:T(4,128)S(1)}, f32[2,6,2048]{2,1,0:T(8,128)S(1)}, f32[3,1024]{1,0:T(4,128)S(1)},...) while((s32[]{:T(128)}, f32[2,6,2048]{2,1,0:T(8,128)S(1)}, ...), condition=%wide.region_56.57_spmd, body=%wide.region_49.56_spmd.sunk | while | flops 85970952 | bytes 499925 | solution.py:37
  1251.1 16.8 fusion.193
  1268.8 16.8 fusion.193
  1286.4 24.9 %all-reduce.35.cloned.1.call-done = f32[6,4096]{1,0:T(8,128)} async-done(((f32[6,4096]{1,0:T(8,128)}), f32[6,4096]{1,0:T(8,128)}) %all-reduce.35.cloned.1.call-update) | async-done | bytes 98320 | tf_op jit(solution)/shard_map/psum | solution.py:96
  1317.3 78.6 %all-reduce.37.cloned.1.call-done = f32[6,4096]{1,0:T(8,128)} async-done(((f32[6,4096]{1,0:T(8,128)}), f32[6,4096]{1,0:T(8,128)}) %all-reduce.37.cloned.1.call-update) | async-done | bytes 98320 | tf_op jit(solution)/shard_map/psum | solution.py:96
  1396.0 32.9 %while.86 = (s32[]{:T(128)}, f32[2,6,2048]{2,1,0:T(8,128)S(1)}, f32[3,1024]{1,0:T(4,128)S(1)}, f32[2,6,2048]{2,1,0:T(8,128)S(1)}, f32[3,1024]{1,0:T(4,128)S(1)},...) while((s32[]{:T(128)}, f32[2,6,2048]{2,1,0:T(8,128)S(1)}, ...), condition=%wide.region_74.75_spmd, body=%wide.region_67.74_spmd.sunk | while | flops 85970952 | bytes 499925 | solution.py:37
  1396.1 16.2 fusion.197
  1412.6 16.2 fusion.197
  1429.5 27.0 %all-reduce.39.cloned.1.call-done = f32[6,4096]{1,0:T(8,128)} async-done(((f32[6,4096]{1,0:T(8,128)}), f32[6,4096]{1,0:T(8,128)}) %all-reduce.39.cloned.1.call-update) | async-done | bytes 98320 | tf_op jit(solution)/shard_map/psum | solution.py:96
  1456.7 32.9 %while.87 = (s32[]{:T(128)}, f32[2,6,2048]{2,1,0:T(8,128)S(1)}, f32[3,1024]{1,0:T(4,128)S(1)}, f32[2,6,2048]{2,1,0:T(8,128)S(1)}, f32[3,1024]{1,0:T(4,128)S(1)},...) while((s32[]{:T(128)}, f32[2,6,2048]{2,1,0:T(8,128)S(1)}, ...), condition=%wide.region_84.85_spmd, body=%wide.region_77.84_spmd.sunk | while | flops 85970952 | bytes 499925 | solution.py:37
  1456.9 16.2 fusion.199
  1473.3 16.2 fusion.199
  1492.9 48.3 %all-reduce.41.cloned.1.call-done = f32[6,4096]{1,0:T(8,128)} async-done(((f32[6,4096]{1,0:T(8,128)}), f32[6,4096]{1,0:T(8,128)}) %all-reduce.41.cloned.1.call-update) | async-done | bytes 98320 | tf_op jit(solution)/shard_map/psum | solution.py:96
  1542.0 59.9 %all-reduce.43.cloned.1.call-done = f32[6,4096]{1,0:T(8,128)} async-done(((f32[6,4096]{1,0:T(8,128)}), f32[6,4096]{1,0:T(8,128)}) %all-reduce.43.cloned.1.call-update) | async-done | bytes 98320 | tf_op jit(solution)/shard_map/psum | solution.py:96
  1602.6 83.8 %all-reduce.45.cloned.1.call-done = f32[6,4096]{1,0:T(8,128)} async-done(((f32[6,4096]{1,0:T(8,128)}), f32[6,4096]{1,0:T(8,128)}) %all-reduce.45.cloned.1.call-update) | async-done | bytes 98320 | tf_op jit(solution)/shard_map/psum | solution.py:96
  1688.0 59.0 %all-reduce.47.cloned.1.call-done = f32[6,4096]{1,0:T(8,128)} async-done(((f32[6,4096]{1,0:T(8,128)}), f32[6,4096]{1,0:T(8,128)}) %all-reduce.47.cloned.1.call-update) | async-done | bytes 98320 | tf_op jit(solution)/shard_map/psum | solution.py:96
  (264 shorter events, 85.1 us)
Async XLA Ops:
  7.2 486.8 %all-reduce.17.cloned.1.call-start = ((), (), s32[]{:S(2)}) async-start(), calls=%async_computation | async-start | bytes 262144 | tf_op jit(solution)/shard_map/psum | solution.py:96
  78.7 11.5 copy-start.21
  289.1 0.6 copy-start.5
  289.8 260.3 %all-reduce.19.cloned.1.call-start = ((), (), s32[]{:S(2)}) async-start(), calls=%async_computation.1 | async-start | bytes 262144 | tf_op jit(solution)/shard_map/psum | solution.py:96
  327.7 2.3 copy-start.6
  362.9 0.7 copy-start.7
  396.4 97.4 %copy-start.8 = (f32[2,6,2048]{2,1,0:T(8,128)}, f32[2,6,2048]{2,1,0:T(8,128)S(1)}, u32[]{:S(2)}) copy-start(f32[2,6,2048]{2,1,0:T(8,128)S(1)} %get-tuple-element.238) | copy-start | bytes 294916
  396.6 238.4 %copy-start.14 = (f32[3,1024]{1,0:T(4,128)S(1)}, f32[3,1024]{1,0:T(4,128)}, u32[]{:S(2)}) copy-start(f32[3,1024]{1,0:T(4,128)} %param.23) | copy-start | bytes 36868
  396.6 238.7 %copy-start.15 = (f32[3,1024]{1,0:T(4,128)S(1)}, f32[3,1024]{1,0:T(4,128)}, u32[]{:S(2)}) copy-start(f32[3,1024]{1,0:T(4,128)} %param.25) | copy-start | bytes 36868
  396.6 238.9 %copy-start.16 = (f32[3,1024]{1,0:T(4,128)S(1)}, f32[3,1024]{1,0:T(4,128)}, u32[]{:S(2)}) copy-start(f32[3,1024]{1,0:T(4,128)} %param.24) | copy-start | bytes 36868
  396.6 239.7 %copy-start.17 = (f32[3,1024]{1,0:T(4,128)S(1)}, f32[3,1024]{1,0:T(4,128)}, u32[]{:S(2)}) copy-start(f32[3,1024]{1,0:T(4,128)} %param.26) | copy-start | bytes 36868
  494.0 140.7 %all-reduce.21.cloned.1.call-start = ((), (), s32[]{:S(2)}) async-start(), calls=%async_computation.2 | async-start | bytes 262144 | tf_op jit(solution)/shard_map/psum | solution.py:96
  550.1 145.3 %all-reduce.23.cloned.1.call-start = ((), (), s32[]{:S(2)}) async-start(), calls=%async_computation.3 | async-start | bytes 262144 | tf_op jit(solution)/shard_map/psum | solution.py:96
  634.8 145.1 %all-reduce.25.cloned.1.call-start = ((), (), s32[]{:S(2)}) async-start(), calls=%async_computation.4 | async-start | bytes 262144 | tf_op jit(solution)/shard_map/psum | solution.py:96
  695.4 145.1 %all-reduce.27.cloned.1.call-start = ((), (), s32[]{:S(2)}) async-start(), calls=%async_computation.5 | async-start | bytes 262144 | tf_op jit(solution)/shard_map/psum | solution.py:96
  695.4 370.9 %copy-start.18 = (s32[1024]{0:T(1024)}, s32[1024]{0:T(1024)S(1)}, u32[]{:S(2)}) copy-start(s32[1024]{0:T(1024)S(1)} %pad_clamp_fusion) | copy-start | bytes 12292
  779.9 145.3 %all-reduce.29.cloned.1.call-start = ((), (), s32[]{:S(2)}) async-start(), calls=%async_computation.6 | async-start | bytes 262144 | tf_op jit(solution)/shard_map/psum | solution.py:96
  840.5 145.4 %all-reduce.31.cloned.1.call-start = ((), (), s32[]{:S(2)}) async-start(), calls=%async_computation.7 | async-start | bytes 262144 | tf_op jit(solution)/shard_map/psum | solution.py:96
  925.2 325.5 %all-reduce.33.cloned.1.call-start = ((), (), s32[]{:S(2)}) async-start(), calls=%async_computation.8 | async-start | bytes 262144 | tf_op jit(solution)/shard_map/psum | solution.py:96
  988.4 77.9 %copy-start.2 = (f32[3,1024]{0,1:T(8,128)}, f32[3,1024]{0,1:T(8,128)S(1)}, u32[]{:S(2)}) copy-start(f32[3,1024]{0,1:T(8,128)S(1)} %scatter_fusion) | copy-start | bytes 36868
  990.0 76.4 %copy-start = (f32[3,1024]{0,1:T(8,128)}, f32[3,1024]{0,1:T(8,128)S(1)}, u32[]{:S(2)}) copy-start(f32[3,1024]{0,1:T(8,128)S(1)} %scatter_fusion.3) | copy-start | bytes 36868
  1170.4 0.6 copy-start.9
  1171.0 140.2 %all-reduce.35.cloned.1.call-start = ((), (), s32[]{:S(2)}) async-start(), calls=%async_computation.9 | async-start | bytes 262144 | tf_op jit(solution)/shard_map/psum | solution.py:96
  1250.7 145.3 %all-reduce.37.cloned.1.call-start = ((), (), s32[]{:S(2)}) async-start(), calls=%async_computation.10 | async-start | bytes 262144 | tf_op jit(solution)/shard_map/psum | solution.py:96
  1286.4 24.9 %copy-start.10 = (f32[2,6,2048]{2,1,0:T(8,128)}, f32[2,6,2048]{2,1,0:T(8,128)S(1)}, u32[]{:S(2)}) copy-start(f32[2,6,2048]{2,1,0:T(8,128)S(1)} %get-tuple-element.242) | copy-start | bytes 294916
  1311.3 145.3 %all-reduce.39.cloned.1.call-start = ((), (), s32[]{:S(2)}) async-start(), calls=%async_computation.11 | async-start | bytes 262144 | tf_op jit(solution)/shard_map/psum | solution.py:96
  1396.0 145.3 %all-reduce.41.cloned.1.call-start = ((), (), s32[]{:S(2)}) async-start(), calls=%async_computation.12 | async-start | bytes 262144 | tf_op jit(solution)/shard_map/psum | solution.py:96
  1428.9 27.7 %copy-start.11 = (f32[2,6,2048]{2,1,0:T(8,128)}, f32[2,6,2048]{2,1,0:T(8,128)S(1)}, u32[]{:S(2)}) copy-start(f32[2,6,2048]{2,1,0:T(8,128)S(1)} %get-tuple-element.245) | copy-start | bytes 294916
  1456.6 145.3 %all-reduce.43.cloned.1.call-start = ((), (), s32[]{:S(2)}) async-start(), calls=%async_computation.13 | async-start | bytes 262144 | tf_op jit(solution)/shard_map/psum | solution.py:96
  1456.7 33.0 %copy-start.1 = (f32[3,1024]{0,1:T(8,128)S(1)}, f32[3,1024]{0,1:T(8,128)}, u32[]{:S(2)}) copy-start(f32[3,1024]{0,1:T(8,128)} %copy-done) | copy-start | bytes 36868
  1456.7 33.0 %copy-start.19 = (s32[1024]{0:T(1024)S(1)}, s32[1024]{0:T(1024)}, u32[]{:S(2)}) copy-start(s32[1024]{0:T(1024)} %copy-done.18) | copy-start | bytes 12292
  1456.7 34.4 %copy-start.3 = (f32[3,1024]{0,1:T(8,128)S(1)}, f32[3,1024]{0,1:T(8,128)}, u32[]{:S(2)}) copy-start(f32[3,1024]{0,1:T(8,128)} %copy-done.2) | copy-start | bytes 36868
  1456.7 84.6 %copy-start.12 = (f32[6,4096]{1,0:T(8,128)S(1)}, f32[6,4096]{1,0:T(8,128)}, u32[]{:S(2)}) copy-start(f32[6,4096]{1,0:T(8,128)} %all-reduce.35.cloned.1.call-done) | copy-start | bytes 294916
  1456.7 145.2 %copy-start.13 = (f32[6,4096]{1,0:T(8,128)S(1)}, f32[6,4096]{1,0:T(8,128)}, u32[]{:S(2)}) copy-start(f32[6,4096]{1,0:T(8,128)} %all-reduce.39.cloned.1.call-done) | copy-start | bytes 294916
  1456.7 292.4 %copy-start.22 = (f32[256]{0:T(256)S(1)}, f32[256]{0:T(256)}, u32[]{:S(2)}) copy-start(f32[256]{0:T(256)} %get-tuple-element.731) | copy-start | bytes 3076
  1456.7 292.4 %copy-start.23 = (f32[256]{0:T(256)S(1)}, f32[256]{0:T(256)}, u32[]{:S(2)}) copy-start(f32[256]{0:T(256)} %get-tuple-element.732) | copy-start | bytes 3076
  1456.7 293.4 %copy-start.20 = (s32[256,1]{0,1:T(1,128)S(1)}, s32[256,1]{0,1:T(1,128)}, u32[]{:S(2)}) copy-start(s32[256,1]{0,1:T(1,128)} %get-tuple-element.729) | copy-start | bytes 3076
  1489.6 112.2 %copy-start.4 = (f32[2,6,2048]{2,1,0:T(8,128)}, f32[2,6,2048]{2,1,0:T(8,128)S(1)}, u32[]{:S(2)}) copy-start(f32[2,6,2048]{2,1,0:T(8,128)S(1)} %get-tuple-element.248) | copy-start | bytes 294916
  1541.3 145.1 %all-reduce.45.cloned.1.call-start = ((), (), s32[]{:S(2)}) async-start(), calls=%async_computation.14 | async-start | bytes 262144 | tf_op jit(solution)/shard_map/psum | solution.py:96
  1601.9 145.1 %all-reduce.47.cloned.1.call-start = ((), (), s32[]{:S(2)}) async-start(), calls=%async_computation.15 | async-start | bytes 262144 | tf_op jit(solution)/shard_map/psum | solution.py:96
Sparse Core Ops, SparseCore 0:
  289.9 79.0 all-reduce.16
  494.1 55.8 all-reduce.18
  553.3 81.4 all-reduce.20
  637.0 58.2 all-reduce.22
  698.4 81.4 all-reduce.24
  782.1 58.2 all-reduce.26
  843.7 81.4 all-reduce.28
  927.6 58.2 all-reduce.30
  1171.2 79.4 all-reduce.32
  1252.9 58.2 all-reduce.34
  1314.5 81.4 all-reduce.36
  1398.2 58.2 all-reduce.38
  1459.8 81.4 all-reduce.40
  1543.5 58.2 all-reduce.42
  1604.9 81.4 all-reduce.44
  1688.7 58.2 all-reduce.46
